TPU v7x, 128 devices: a whole 4x4x4 slice. The times are simulated.
128 devices in a mesh: tok: 8 (over z, y_hi), head: 16 (over x, y_lo, core).
Axes of the slice: x: 4, y: 4 (y_hi: 2, y_lo: 2; y = y_hi * 2 + y_lo), z: 4, core: 2. Of those that a mesh axis runs over, the one named last changes fastest.
Arguments:
- states: bfloat16 [4096, 4096], P('tok', 'head'), may hold values from -400 to 400
- pre_gain: float32 [4096], replicated, may hold values from 0.5 to 1.5
- pre_shift: float32 [4096], replicated, may hold values from -1.75 to 1.75
- mlp_gain: float32 [4096], replicated, may hold values from 0.5 to 1.5
- mlp_shift: float32 [4096], replicated, may hold values from -1.75 to 1.75
- qkv_weight: bfloat16 [4096, 12288], P('tok', 'head'), may hold values from -0.09375 to 0.09375
- qkv_bias: float32 [12288], P('head'), may hold values from -1.75 to 1.75
- out_weight: bfloat16 [4096, 4096], P('head', 'tok'), may hold values from -0.125 to 0.125
- out_bias: float32 [4096], P('head'), may hold values from -1.75 to 1.75
- up_weight: bfloat16 [4096, 16384], P(None, 'head'), may hold values from -0.09375 to 0.09375
- up_bias: float32 [16384], P('head'), may hold values from -1.75 to 1.75
- down_weight: bfloat16 [16384, 4096], P('head'), may hold values from -0.0625 to 0.0625
- down_bias: float32 [4096], P('head'), may hold values from -1.75 to 1.75
- kv_cache: bfloat16 [1152, 2, 16, 4096], P(('tok', 'head')), may hold values from -320 to 320, as said below
- token_request: int32 [4096], P('tok'), may hold values from 0 to 15, as said below
- cached_len: int32 [16], P('tok'), may hold values from 128 to 1024, as said below
- page_table: int32 [16, 64], P('tok'), may hold values from 0 to 143, as said below
- migrations: int32 [64, 2], P('tok'), may hold values from 0 to 143, as said below
Outputs:
- update: bfloat16 [4096, 4096], P('tok', 'head')
Inputs may be any that keep to these rules, and one draw needn't show every extreme that they name: `token_request`: ids never fall; the tokens of request r lie among tokens (r // 2) * 512 to that plus 512 - 1, and every request has one token or more. `cached_len`: some request holds exactly 1024. `page_table`: the entries of one block are distinct. `migrations`: targets of one block are distinct and none is also a source of that block. `kv_cache`: keys are stored already rotated.
All inputs are finite; a program needn't handle non-finite values.
Results may differ from a plain program's by a relative error of at most 0.018.
The roundings to bfloat16 on the way count: a program that leaves them out, or rounds other values in their place, can miss the bound.
Values may be sent and summed in bfloat16 or wider, within the bound.
No kernel may reach another device: no remote copies, remote signals or barrier semaphores. Data moves between devices by JAX's collectives and lax.ppermute only.
A program may use at most 128 MiB of HBM per device.

v0:
```python
import jax
import jax.numpy as jnp
from jax import lax
from jax.sharding import PartitionSpec as P

HD = 128
ROT = 32
epsilon = 1e-05


def layer_norm(wide, gain, shift):
    row_mean = jnp.mean(wide, axis=1, keepdims=True)
    centred = wide - row_mean
    row_var = jnp.mean(centred * centred, axis=1, keepdims=True)
    return (centred * lax.rsqrt(row_var + epsilon) * gain + shift).astype(jnp.bfloat16)


def rotate(vectors, positions):
    half_rot = ROT // 2
    inv_freq = 10000.0 ** (-2.0 * jnp.arange(half_rot, dtype=jnp.float32) / ROT)
    angles = positions.astype(jnp.float32)[:, None] * inv_freq[None, :]
    cosine = jnp.cos(angles)[:, None, :]
    sine_part = jnp.sin(angles)[:, None, :]
    lower_half = vectors[..., :half_rot]
    upper_half = vectors[..., half_rot:ROT]
    return jnp.concatenate(
        [
            lower_half * cosine - upper_half * sine_part,
            upper_half * cosine + lower_half * sine_part,
            vectors[..., ROT:],
        ],
        axis=-1,
    )


def token_positions(local_req, cached):
    onehot = local_req[:, None] == jnp.arange(cached.shape[0], dtype=jnp.int32)[None, :]
    stretch_sizes = jnp.sum(onehot.astype(jnp.int32), axis=0)
    starts = jnp.cumsum(stretch_sizes) - stretch_sizes
    own_start = jnp.sum(jnp.where(onehot, starts[None, :], 0), axis=1)
    own_cached = jnp.sum(jnp.where(onehot, cached[None, :], 0), axis=1)
    return own_cached + jnp.arange(local_req.shape[0], dtype=jnp.int32) - own_start


def attend(queries, new_keys, new_values, cache_keys, cache_values, local_req, cached, positions):
    span = cache_keys.shape[0] // cached.shape[0]
    key_slot = jnp.arange(cache_keys.shape[0], dtype=jnp.int32)
    key_owner = key_slot // span
    key_place = key_slot % span
    cache_ok = (local_req[:, None] == key_owner[None, :]) & (
        key_place[None, :] < jnp.repeat(cached, span)[None, :]
    )
    new_ok = (local_req[:, None] == local_req[None, :]) & (positions[None, :] <= positions[:, None])
    allowed = jnp.concatenate([cache_ok, new_ok], axis=1)
    all_keys = jnp.concatenate([cache_keys, new_keys], axis=0)
    all_values = jnp.concatenate([cache_values, new_values], axis=0)
    scores = jnp.einsum(
        "thd,khd->htk", queries, all_keys, preferred_element_type=jnp.float32
    ) * HD ** (-0.5)
    scores = jnp.where(allowed[None], scores, -1e30)
    peak = jnp.max(scores, axis=2, keepdims=True)
    exp_scores = jnp.exp(scores - peak)
    attn_probs = (exp_scores / jnp.sum(exp_scores, axis=2, keepdims=True)).astype(jnp.bfloat16)
    return jnp.einsum(
        "htk,khd->thd", attn_probs, all_values, preferred_element_type=jnp.float32
    ).astype(jnp.bfloat16)


def share_pages(local_pool, groups):
    grouped = local_pool.reshape(
        local_pool.shape[0], 2, local_pool.shape[2], groups, local_pool.shape[3] // groups
    )
    shared = lax.all_to_all(grouped, "head", split_axis=3, concat_axis=0, tiled=True)
    return shared.reshape(shared.shape[0], 2, shared.shape[2], shared.shape[4])


def shards(
    states,
    pre_gain,
    pre_shift,
    mlp_gain,
    mlp_shift,
    qkv_weight,
    qkv_bias,
    out_weight,
    out_bias,
    up_weight,
    up_bias,
    down_weight,
    down_bias,
    kv_cache,
    token_request,
    cached_len,
    page_table,
    migrations,
):
    gathered = lax.all_gather(states, "head", axis=1, tiled=True)
    wide = gathered.astype(jnp.float32)
    pre_normed = layer_norm(wide, pre_gain, pre_shift)
    mlp_normed = layer_norm(wide, mlp_gain, mlp_shift)
    tok_rows = gathered.shape[0]
    joined = jnp.dot(
        pre_normed,
        lax.all_gather(qkv_weight, "tok", axis=0, tiled=True),
        preferred_element_type=jnp.float32,
    )
    joined = (joined + qkv_bias).reshape(tok_rows, -1, 3, HD)
    local_req = token_request - lax.axis_index("tok") * cached_len.shape[0]
    positions = token_positions(local_req, cached_len)
    queries = rotate(joined[:, :, 0], positions).astype(jnp.bfloat16)
    new_keys = rotate(joined[:, :, 1], positions).astype(jnp.bfloat16)
    new_values = joined[:, :, 2].astype(jnp.bfloat16)
    head_groups = lax.axis_size("head")
    pool_size = kv_cache.shape[0]
    sources = migrations[:, 0]
    targets = migrations[:, 1]
    own_index = lax.axis_index("head")
    owner_mask = sources // pool_size == own_index
    picked = jnp.where(
        owner_mask[:, None, None, None], kv_cache[sources % pool_size], jnp.zeros((), jnp.bfloat16)
    )
    moved_pages = lax.psum(picked, "head").astype(jnp.float32).astype(jnp.bfloat16)
    landing = jnp.where(targets // pool_size == own_index, targets % pool_size, pool_size)
    local_pool = kv_cache.at[landing].set(moved_pages, mode="drop")
    page_pool = share_pages(local_pool, head_groups)
    pages = page_pool[page_table.reshape(-1)]
    cache_keys = pages[:, 0].reshape(-1, queries.shape[1], HD)
    cache_values = pages[:, 1].reshape(-1, queries.shape[1], HD)
    heads_out = attend(
        queries, new_keys, new_values, cache_keys, cache_values, local_req, cached_len, positions
    ).reshape(tok_rows, -1)
    attention_part = jnp.dot(
        heads_out,
        lax.all_gather(out_weight, "tok", axis=1, tiled=True),
        preferred_element_type=jnp.float32,
    )
    hidden = jax.nn.gelu(
        jnp.dot(mlp_normed, up_weight, preferred_element_type=jnp.float32) + up_bias,
        approximate=False,
    ).astype(jnp.bfloat16)
    feed_part = jnp.dot(hidden, down_weight, preferred_element_type=jnp.float32)
    summed = lax.psum_scatter(
        (attention_part + feed_part).astype(jnp.bfloat16), "head", scatter_dimension=1, tiled=True
    ).astype(jnp.float32)
    return (summed + out_bias + down_bias).astype(jnp.bfloat16)


def solution(mesh):
    in_specs = (
        P("tok", "head"),
        P(),
        P(),
        P(),
        P(),
        P("tok", "head"),
        P("head"),
        P("head", "tok"),
        P("head"),
        P(None, "head"),
        P("head"),
        P("head", None),
        P("head"),
        P(("tok", "head"), None, None, None),
        P("tok"),
        P("tok"),
        P("tok", None),
        P("tok", None),
    )
    out_specs = P("tok", "head")
    return jax.shard_map(shards, mesh=mesh, in_specs=in_specs, out_specs=out_specs, check_vma=False)
```

profile of v0, /device:TPU:0, one launch (start us, length us, event | category | flops | bytes accessed | tf_op | source)
XLA Modules:
  0.0 436.5 jit_solution(8468783990483172287)
XLA Ops:
  6.5 1.7 copy.59
  8.3 2.0 gather_fusion
  10.3 3.1 broadcast_select_fusion
  15.9 123.9 %all-reduce.2.cloned.1.call-done = bf16[8,2,16,4096]{3,2,1,0:T(8,128)(2,1)} async-done(((bf16[8,2,16,4096]{3,2,1,0:T(8,128)(2,1)}), bf16[8,2,16,4096]{3,2,1,0:T(8,128)(2,1)}) %all-reduce.2.cloned.1.call-update) | async-done | bytes 2097168 | tf_op jit(solution)/shard_map/psum | solution.py:122
  139.8 3.2 scatter_fusion
  143.1 1.8 copy.55
  144.8 4.8 %all-to-all-start = ((bf16[9,2,16,16,256]{4,2,1,0,3:T(8,128)(2,1)}), bf16[9,2,16,16,256]{4,2,1,0,3:T(8,128)(2,1)S(1)}, u32[]{:S(2)}, u32[]{:S(2)}) async-start(bf16[9,2,16,16,256]{4,2,1,0,3:T(8,128)(2,1)} %bitcast.48), calls=%async_computation | async-start | bytes 4718592 | tf_op jit(solution)/shard_map/all_to_all | solution.py:73
  150.0 0.8 copy.42
  151.3 0.7 compare_and_fusion
  152.1 1.2 pad_add_fusion
  153.3 33.0 %all-to-all-done = bf16[9,2,16,16,256]{4,2,1,0,3:T(8,128)(2,1)S(1)} async-done(((bf16[9,2,16,16,256]{4,2,1,0,3:T(8,128)(2,1)}), bf16[9,2,16,16,256]{4,2,1,0,3:T(8,128)(2,1)S(1)}, u32[]{:S(2)}, u32[]{:S(2)}) %all-to-all-start) | async-done | bytes 2359328 | tf_op jit(solution)/shard_map/all_to_all | solution.py:73
  186.3 2.0 gather_fusion.1
  188.3 1.7 fusion.146
  190.3 1.2 copy.44
  191.8 2.1 copy.39
  193.8 16.8 %all-gather.4.cloned.1.call-done = bf16[512,4096]{1,0:T(8,128)(2,1)} async-done(((bf16[512,256]{1,0:T(8,128)(2,1)}), bf16[512,4096]{1,0:T(8,128)(2,1)}) %all-gather.4.cloned.1.call-update) | async-done | bytes 4194320 | tf_op jit(solution)/shard_map/all_gather | solution.py:97
  210.6 3.0 convert_reduce_fusion
  214.1 1.2 fusion.9
  215.4 24.2 %fusion.40 = f32[512,4096]{1,0:T(8,128)} fusion(bf16[1024,4096]{1,0:T(8,128)(2,1)} %param.29, bf16[4096,1024]{1,0:T(8,128)(2,1)} %param.27, bf16[512,4096]{1,0:T(8,128)(2,1)} %all-gather.4.cloned.1.call-done, f32[4096]{0:T(1024)S(1)} %copy-done.9, f32[4096]{0:T(1024)S(1)} %copy-done.10, f32[512]{0:T(512)S(1)} %add_rsqrt_fusion, ...), kind=kOutput, calls=%fused_computation.57 | convolution fusion | flops 8637120512 | bytes 29401088 | tf_op jit(solution)/shard_map/dot_general | solution.py:141
  239.5 61.8 %all-gather.6.cloned.1.call-done = bf16[4096,768]{1,0:T(8,128)(2,1)} async-done(((bf16[512,768]{1,0:T(8,128)(2,1)}), bf16[4096,768]{1,0:T(8,128)(2,1)}) %all-gather.6.cloned.1.call-update) | async-done | bytes 6291472 | tf_op jit(solution)/shard_map/all_gather | solution.py:104
  301.3 9.1 %fusion.42 = f32[512,768]{1,0:T(8,128)} fusion(bf16[4096,768]{1,0:T(8,128)(2,1)} %all-gather.6.cloned.1.call-done, bf16[512,4096]{1,0:T(8,128)(2,1)} %all-gather.4.cloned.1.call-done, f32[4096]{0:T(1024)S(1)} %copy-done.11, f32[4096]{0:T(1024)S(1)} %copy-done.12, f32[512]{0:T(512)S(1)} %add_rsqrt_fusion, f32[512]{0:T(512)S(1)} %broadcast_multiply_fusion, ...), kind=kOutput, calls=%fused_computation.58 | convolution fusion | flops 3234201600 | bytes 12098560 | tf_op jit(solution)/shard_map/dot_general | solution.py:102
  310.4 1.9 copy.37
  312.8 0.8 slice.83
  313.7 0.9 slice.84
  314.5 0.7 fusion.94
  315.3 2.2 subtract_convert_fusion.1
  317.4 10.0 %fusion.148 = (f32[2,512]{1,0:T(2,128)S(1)}, f32[2,512,2560]{2,1,0:T(8,128)}) fusion(pred[512,2560]{1,0:T(8,128)(4,1)S(1)} %copy-done.1, bf16[512,2,96]{2,0,1:T(8,128)(2,1)} %slice.83, bf16[512,2,16]{2,0,1:T(8,128)(2,1)S(1)} %get-tuple-element.17, bf16[512,2,16]{2,0,1:T(8,128)(2,1)} %get-tuple-element.18, bf16[2048,2,128]{2,0,1:T(8,128)(2,1)} %copy.44, ...), kind=kOutput, calls=%fused_computation.190 | convolution fusion | flops 687606272 | bytes 13373440 | tf_op jit(solution)/shard_map/sub | solution.py:62
  327.4 5.9 %fusion.56 = bf16[2,128,512]{2,1,0:T(8,128)(2,1)S(1)} fusion(f32[2,512,2560]{2,1,0:T(8,128)} %get-tuple-element.24, f32[2,512]{1,0:T(2,128)S(1)} %get-tuple-element.23, bf16[512,2,128]{0,2,1:T(8,128)(2,1)S(1)} %copy-done.3, bf16[2048,2,128]{0,2,1:T(8,128)(2,1)S(1)} %copy-done.2), kind=kOutput, calls=%fused_computation.70 | convolution fusion | flops 679084032 | bytes 12062720 | tf_op jit(solution)/shard_map/htk,khd->thd/dot_general | solution.py:64
  333.3 22.3 %all-gather.8.cloned.1.call-done = bf16[256,4096]{1,0:T(8,128)(2,1)} async-done(((bf16[256,512]{1,0:T(8,128)(2,1)}), bf16[256,4096]{1,0:T(8,128)(2,1)}) %all-gather.8.cloned.1.call-update) | async-done | bytes 2097168 | tf_op jit(solution)/shard_map/all_gather | solution.py:134
  355.7 7.2 %add_convert_fusion = bf16[512,4096]{1,0:T(8,128)(2,1)} fusion(f32[512,4096]{1,0:T(8,128)} %fusion.40, bf16[512,256]{0,1:T(8,128)(2,1)S(1)} %bitcast.56, bf16[256,4096]{1,0:T(8,128)(2,1)} %all-gather.8.cloned.1.call-done), kind=kOutput, calls=%fused_computation.18 | convolution fusion | flops 1077936128 | bytes 14942208 | tf_op jit(solution)/shard_map/dot_general | solution.py:132
  362.9 65.4 %reduce-scatter.2.cloned.1.call-done = bf16[512,256]{1,0:T(8,128)(2,1)} async-done(((bf16[512,4096]{1,0:T(8,128)(2,1)}), bf16[512,256]{1,0:T(8,128)(2,1)}) %reduce-scatter.2.cloned.1.call-update) | async-done | bytes 262160 | tf_op jit(solution)/shard_map/reduce_scatter | solution.py:142
  428.3 1.7 add_convert_fusion.1
  (68 shorter events, 4.9 us)
Async XLA Ops:
  6.5 1.7 copy-start.8
  6.5 133.3 %all-reduce.2.cloned.1.call-start = ((), (), s32[]{:S(2)}) async-start(), calls=%async_computation.2 | async-start | bytes 4194304 | tf_op jit(solution)/shard_map/psum | solution.py:122
  13.4 2.1 copy-start.5
  13.4 2.4 copy-start.4
  13.4 197.2 %all-gather.4.cloned.1.call-start = ((), (), s32[]{:S(2)}) async-start(), calls=%async_computation.3 | async-start | bytes 4456448 | tf_op jit(solution)/shard_map/all_gather | solution.py:97
  14.2 287.1 %all-gather.6.cloned.1.call-start = ((), (), s32[]{:S(2)}) async-start(), calls=%async_computation.4 | async-start | bytes 7077888 | tf_op jit(solution)/shard_map/all_gather | solution.py:104
  14.9 340.7 %all-gather.8.cloned.1.call-start = ((), (), s32[]{:S(2)}) async-start(), calls=%async_computation.5 | async-start | bytes 2359296 | tf_op jit(solution)/shard_map/all_gather | solution.py:134
  144.8 6.0 %copy-start.15 = (s32[2,64]{1,0:T(2,128)S(1)}, s32[2,64]{1,0:T(2,128)}, u32[]{:S(2)}) copy-start(s32[2,64]{1,0:T(2,128)} %param.34) | copy-start | bytes 1540
  144.8 41.5 %all-to-all-start = ((bf16[9,2,16,16,256]{4,2,1,0,3:T(8,128)(2,1)}), bf16[9,2,16,16,256]{4,2,1,0,3:T(8,128)(2,1)S(1)}, u32[]{:S(2)}, u32[]{:S(2)}) async-start(bf16[9,2,16,16,256]{4,2,1,0,3:T(8,128)(2,1)} %bitcast.48), calls=%async_computation | async-start | bytes 4718592 | tf_op jit(solution)/shard_map/all_to_all | solution.py:73
  149.6 278.7 %reduce-scatter.2.cloned.1.call-start = ((), (), s32[]{:S(2)}) async-start(), calls=%async_computation.6 | async-start | bytes 4456448 | tf_op jit(solution)/shard_map/reduce_scatter | solution.py:142
  210.6 3.4 copy-start
  214.0 1.2 copy-start.9
  214.1 1.2 copy-start.10
  214.1 1.3 copy-start.13
  215.3 86.0 %copy-start.11 = (f32[4096]{0:T(1024)S(1)}, f32[4096]{0:T(1024)}, u32[]{:S(2)}) copy-start(f32[4096]{0:T(1024)} %param.20) | copy-start | bytes 49156
  215.3 85.9 %copy-start.12 = (f32[4096]{0:T(1024)S(1)}, f32[4096]{0:T(1024)}, u32[]{:S(2)}) copy-start(f32[4096]{0:T(1024)} %param.19) | copy-start | bytes 49156
  215.3 85.9 %copy-start.14 = (f32[768]{0:T(1024)S(1)}, f32[768]{0:T(1024)}, u32[]{:S(2)}) copy-start(f32[768]{0:T(1024)} %param.24) | copy-start | bytes 9220
  315.3 2.2 copy-start.1
  317.4 10.0 %copy-start.2 = (bf16[2048,2,128]{0,2,1:T(8,128)(2,1)S(1)}, bf16[2048,2,128]{0,2,1:T(8,128)(2,1)}, u32[]{:S(2)}) copy-start(bf16[2048,2,128]{0,2,1:T(8,128)(2,1)} %copy.39) | copy-start | bytes 3145732
  317.4 10.0 %copy-start.3 = (bf16[512,2,128]{0,2,1:T(8,128)(2,1)S(1)}, bf16[512,2,128]{0,2,1:T(8,128)(2,1)}, u32[]{:S(2)}) copy-start(bf16[512,2,128]{0,2,1:T(8,128)(2,1)} %fusion.94) | copy-start | bytes 786436
  362.9 65.4 %copy-start.6 = (f32[256]{0:T(256)S(1)}, f32[256]{0:T(256)}, u32[]{:S(2)}) copy-start(f32[256]{0:T(256)} %param.30) | copy-start | bytes 3076
  362.9 65.4 %copy-start.7 = (f32[256]{0:T(256)S(1)}, f32[256]{0:T(256)}, u32[]{:S(2)}) copy-start(f32[256]{0:T(256)} %param.26) | copy-start | bytes 3076
Sparse Core Ops, SparseCore 0:
  13.6 126.1 all-reduce.1
  141.4 69.1 all-gather.3
  212.9 88.3 all-gather.5
  303.3 52.3 all-gather.7
  363.1 65.1 reduce-scatter.1
where the time goes:
time: 437 us
  waiting for transfers between devices  325 us (74%)
  matrix products  56.4 us (13%)
  local copies, waits for them, and re-layouts  22.7 us (5%)
  other arithmetic  14.1 us (3%)
  between operations  13.4 us (3%)
  starting transfers between devices  4.96 us (1%)
    psum x1, waiting for transfers between devices, shards(): lax.psum(picked, 'head').astype(jnp.float32).astype(jnp.bfloat16)  124 us
    reduce_scatter x1, waiting for transfers between devices, shards(): lax.psum_scatter((attention_part + feed_part).astype(jnp.bfloat16), 'head...  65.4 us
    all_gather x1, waiting for transfers between devices, shards(): lax.all_gather(qkv_weight, 'tok', axis=0, tiled=True)  61.8 us
    all_to_all x1, waiting for transfers between devices, share_pages(): lax.all_to_all(grouped, 'head', split_axis=3, concat_axis=0, tiled=True)  33 us
    dot_general x1, matrix products, shards(): feed_part = jnp.dot(hidden, down_weight, preferred_element_type=jnp.float32)  24.2 us
    all_gather x1, waiting for transfers between devices, shards(): lax.all_gather(out_weight, 'tok', axis=1, tiled=True)  22.3 us
    all_gather x1, waiting for transfers between devices, shards(): gathered = lax.all_gather(states, 'head', axis=1, tiled=True)  16.8 us
    sub x1, matrix products, attend(): exp_scores = jnp.exp(scores - peak)  9.97 us
  transfers between devices with their start and end apart: 6, of which 6 were waited for; matrix products, arithmetic and copies ran while one was open for 18% of the time, Pallas kernels for 0%

commit v1 on v0

--- a/solution.py
+++ b/solution.py
@@ -119,7 +119,9 @@
     picked = jnp.where(
         owner_mask[:, None, None, None], kv_cache[sources % pool_size], jnp.zeros((), jnp.bfloat16)
     )
-    moved_pages = lax.psum(picked, "head").astype(jnp.float32).astype(jnp.bfloat16)
+    moved_pages = (
+        jnp.sum(lax.all_gather(picked, "head"), axis=0).astype(jnp.float32).astype(jnp.bfloat16)
+    )
     landing = jnp.where(targets // pool_size == own_index, targets % pool_size, pool_size)
     local_pool = kv_cache.at[landing].set(moved_pages, mode="drop")
     page_pool = share_pages(local_pool, head_groups)

time: 437 us -> 465 us (1.064)
  other arithmetic: 14.1 us -> 27.4 us
  waiting for transfers between devices: 325 us -> 334 us
  local copies, waits for them, and re-layouts: 22.7 us -> 28.7 us
    all_gather x0 -> x1, waiting for transfers between devices: none -> 168 us  [shards(): lax.all_gather(picked, 'head')]
    psum x1 -> x0, waiting for transfers between devices: 124 us -> none  [shards(): lax.psum(picked, 'head').astype(jnp.float32).astype(jnp.bfloat16)]
    all_to_all x1, waiting for transfers between devices: 33 us -> 0.01 us  [share_pages(): lax.all_to_all(grouped, 'head', split_axis=3, concat_axis=0, tiled=True)]
    all_gather x1, waiting for transfers between devices: 16.8 us -> 36.8 us  [shards(): gathered = lax.all_gather(states, 'head', axis=1, tiled=True)]
    all_gather x1, waiting for transfers between devices: 22.3 us -> 8.03 us  [shards(): lax.all_gather(out_weight, 'tok', axis=1, tiled=True)]
    reduce_sum x0 -> x1, other arithmetic: none -> 13 us  [shards(): jnp.sum(lax.all_gather(picked, 'head'), axis=0).astype(jnp.float32)]
    all_gather x1, waiting for transfers between devices: 61.8 us -> 54.4 us  [shards(): lax.all_gather(qkv_weight, 'tok', axis=0, tiled=True)]
  transfers between devices with their start and end apart: 6 -> 6, of which waited for: 6 -> 5; matrix products, arithmetic and copies ran while one was open for 18% -> 22% of each run, Pallas kernels for 0% -> 0%
where the time goes in v1:
time: 465 us
  waiting for transfers between devices  334 us (72%)
  matrix products  56.3 us (12%)
  local copies, waits for them, and re-layouts  28.7 us (6%)
  other arithmetic  27.4 us (6%)
  between operations  13.4 us (3%)
  starting transfers between devices  5.51 us (1%)
    all_gather x1, waiting for transfers between devices, shards(): lax.all_gather(picked, 'head')  168 us
    reduce_scatter x1, waiting for transfers between devices, shards(): lax.psum_scatter((attention_part + feed_part).astype(jnp.bfloat16), 'head...  65.3 us
    all_gather x1, waiting for transfers between devices, shards(): lax.all_gather(qkv_weight, 'tok', axis=0, tiled=True)  54.4 us
    all_gather x1, waiting for transfers between devices, shards(): gathered = lax.all_gather(states, 'head', axis=1, tiled=True)  36.8 us
    dot_general x1, matrix products, shards(): feed_part = jnp.dot(hidden, down_weight, preferred_element_type=jnp.float32)  23.8 us
    reduce_sum x1, other arithmetic, shards(): jnp.sum(lax.all_gather(picked, 'head'), axis=0).astype(jnp.float32)  13 us
    sub x1, matrix products, attend(): exp_scores = jnp.exp(scores - peak)  9.87 us
    dot_general x1, matrix products, shards(): jnp.dot(pre_normed, lax.all_gather(qkv_weight, 'tok', axis=0, tiled=True)...  9.36 us
  transfers between devices with their start and end apart: 6, of which 5 were waited for; matrix products, arithmetic and copies ran while one was open for 22% of the time, Pallas kernels for 0%

profile of v1, /device:TPU:0, one launch (start us, length us, event | category | flops | bytes accessed | tf_op | source)
XLA Modules:
  0.0 464.7 jit_solution(9687319788795904769)
XLA Ops:
  6.5 1.7 copy.65
  8.3 2.0 gather_fusion
  10.4 3.2 bitcast_select_fusion
  16.5 0.9 copy.49
  18.5 1.1 pad_add_fusion
  19.6 36.8 %all-gather.7.cloned.1.call-done = bf16[512,4096]{1,0:T(8,128)(2,1)} async-done(((bf16[512,256]{1,0:T(8,128)(2,1)}), bf16[512,4096]{1,0:T(8,128)(2,1)}) %all-gather.7.cloned.1.call-update) | async-done | bytes 4194320 | tf_op jit(solution)/shard_map/all_gather | solution.py:97
  56.4 3.0 convert_reduce_fusion
  59.9 1.2 fusion.9
  61.1 167.8 %all-gather.5.cloned.1.call-done = bf16[16,8,2,16,4096]{4,3,2,1,0:T(8,128)(2,1)} async-done(((bf16[1,8,2,16,4096]{4,3,2,1,0:T(8,128)(2,1)}), bf16[16,8,2,16,4096]{4,3,2,1,0:T(8,128)(2,1)}) %all-gather.5.cloned.1.call-update) | async-done | bytes 33554448 | tf_op jit(solution)/shard_map/all_gather | solution.py:123
  228.9 13.0 %reduce_sum.74 = bf16[8,2,16,4096]{3,2,1,0:T(8,128)(2,1)} reduce(bf16[16,8,2,16,4096]{4,3,2,1,0:T(8,128)(2,1)} %all-gather.5.cloned.1.call-done, bf16[]{:T(256)} %constant.46.clone.1), dimensions={0}, to_apply=%region_0.0 | reduce | flops 15728640 | bytes 35651584 | tf_op jit(solution)/shard_map/reduce_sum | solution.py:123
  241.9 3.3 scatter_fusion
  245.2 1.7 copy.62
  246.9 5.2 %all-to-all-start = ((bf16[9,2,16,16,256]{4,2,1,0,3:T(8,128)(2,1)}), bf16[9,2,16,16,256]{4,2,1,0,3:T(8,128)(2,1)S(1)}, u32[]{:S(2)}, u32[]{:S(2)}) async-start(bf16[9,2,16,16,256]{4,2,1,0,3:T(8,128)(2,1)} %bitcast.50), calls=%async_computation | async-start | bytes 4718592 | tf_op jit(solution)/shard_map/all_to_all | solution.py:73
  252.4 23.8 %fusion.40 = f32[512,4096]{1,0:T(8,128)} fusion(bf16[1024,4096]{1,0:T(8,128)(2,1)} %param.29, bf16[4096,1024]{1,0:T(8,128)(2,1)} %param.27, bf16[512,4096]{1,0:T(8,128)(2,1)} %all-gather.7.cloned.1.call-done, f32[4096]{0:T(1024)S(1)} %copy-done.9, f32[4096]{0:T(1024)S(1)} %copy-done.10, f32[512]{0:T(512)S(1)} %add_rsqrt_fusion, ...), kind=kOutput, calls=%fused_computation.57 | convolution fusion | flops 8637120512 | bytes 29401088 | tf_op jit(solution)/shard_map/dot_general | solution.py:143
  276.2 54.4 %all-gather.9.cloned.1.call-done = bf16[4096,768]{1,0:T(8,128)(2,1)} async-done(((bf16[512,768]{1,0:T(8,128)(2,1)}), bf16[4096,768]{1,0:T(8,128)(2,1)}) %all-gather.9.cloned.1.call-update) | async-done | bytes 6291472 | tf_op jit(solution)/shard_map/all_gather | solution.py:104
  330.6 9.4 %fusion.42 = f32[512,768]{1,0:T(8,128)} fusion(bf16[4096,768]{1,0:T(8,128)(2,1)} %all-gather.9.cloned.1.call-done, bf16[512,4096]{1,0:T(8,128)(2,1)} %all-gather.7.cloned.1.call-done, f32[4096]{0:T(1024)S(1)} %copy-done.11, f32[4096]{0:T(1024)S(1)} %copy-done.12, f32[512]{0:T(512)S(1)} %add_rsqrt_fusion, f32[512]{0:T(512)S(1)} %broadcast_multiply_fusion, ...), kind=kOutput, calls=%fused_computation.58 | convolution fusion | flops 3234201600 | bytes 12098560 | tf_op jit(solution)/shard_map/dot_general | solution.py:102
  339.9 3.0 copy.44
  343.0 2.1 fusion.147
  345.3 1.2 copy.53
  346.5 0.8 slice.83
  348.2 1.8 fusion.94
  350.0 2.4 subtract_convert_fusion.1
  352.4 2.0 gather_fusion.1
  354.4 1.7 fusion.146
  356.4 1.1 copy.51
  357.8 2.1 copy.46
  359.9 9.9 %fusion.148 = (f32[2,512]{1,0:T(2,128)S(1)}, f32[2,512,2560]{2,1,0:T(8,128)}) fusion(pred[512,2560]{1,0:T(8,128)(4,1)S(1)} %copy-done.1, bf16[512,2,96]{2,0,1:T(8,128)(2,1)} %slice.83, bf16[512,2,16]{2,0,1:T(8,128)(2,1)} %get-tuple-element.17, bf16[512,2,16]{2,0,1:T(8,128)(2,1)} %get-tuple-element.18, bf16[2048,2,128]{2,0,1:T(8,128)(2,1)S(1)} %copy-done.2, ...), kind=kOutput, calls=%fused_computation.190 | convolution fusion | flops 687606272 | bytes 13373440 | tf_op jit(solution)/shard_map/sub | solution.py:62
  369.8 6.0 %fusion.56 = bf16[2,128,512]{2,1,0:T(8,128)(2,1)S(1)} fusion(f32[2,512,2560]{2,1,0:T(8,128)} %get-tuple-element.24, f32[2,512]{1,0:T(2,128)S(1)} %get-tuple-element.23, bf16[512,2,128]{0,2,1:T(8,128)(2,1)} %fusion.94, bf16[2048,2,128]{0,2,1:T(8,128)(2,1)S(1)} %copy-done.3), kind=kOutput, calls=%fused_computation.70 | convolution fusion | flops 679084032 | bytes 12062720 | tf_op jit(solution)/shard_map/htk,khd->thd/dot_general | solution.py:64
  375.8 8.0 %all-gather.11.cloned.1.call-done = bf16[256,4096]{1,0:T(8,128)(2,1)} async-done(((bf16[256,512]{1,0:T(8,128)(2,1)}), bf16[256,4096]{1,0:T(8,128)(2,1)}) %all-gather.11.cloned.1.call-update) | async-done | bytes 2097168 | tf_op jit(solution)/shard_map/all_gather | solution.py:136
  383.9 7.2 %add_convert_fusion = bf16[512,4096]{1,0:T(8,128)(2,1)} fusion(f32[512,4096]{1,0:T(8,128)} %fusion.40, bf16[512,256]{0,1:T(8,128)(2,1)S(1)} %bitcast.58, bf16[256,4096]{1,0:T(8,128)(2,1)} %all-gather.11.cloned.1.call-done), kind=kOutput, calls=%fused_computation.18 | convolution fusion | flops 1077936128 | bytes 14942208 | tf_op jit(solution)/shard_map/dot_general | solution.py:134
  391.1 65.3 %reduce-scatter.2.cloned.1.call-done = bf16[512,256]{1,0:T(8,128)(2,1)} async-done(((bf16[512,4096]{1,0:T(8,128)(2,1)}), bf16[512,256]{1,0:T(8,128)(2,1)}) %reduce-scatter.2.cloned.1.call-update) | async-done | bytes 262160 | tf_op jit(solution)/shard_map/reduce_scatter | solution.py:144
  456.5 1.7 add_convert_fusion.1
  (69 shorter events, 6.4 us)
Async XLA Ops:
  6.5 1.8 copy-start.8
  6.5 49.9 %all-gather.7.cloned.1.call-start = ((), (), s32[]{:S(2)}) async-start(), calls=%async_computation.3 | async-start | bytes 4456448 | tf_op jit(solution)/shard_map/all_gather | solution.py:97
  8.2 220.7 %all-gather.5.cloned.1.call-start = ((), (), s32[]{:S(2)}) async-start(), calls=%async_computation.2 | async-start | bytes 35651584 | tf_op jit(solution)/shard_map/all_gather | solution.py:123
  13.5 1.4 copy-start.5
  13.5 1.7 copy-start.4
  13.6 4.1 copy-start.15
  13.6 317.0 %all-gather.9.cloned.1.call-start = ((), (), s32[]{:S(2)}) async-start(), calls=%async_computation.4 | async-start | bytes 7077888 | tf_op jit(solution)/shard_map/all_gather | solution.py:104
  14.3 369.5 %all-gather.11.cloned.1.call-start = ((), (), s32[]{:S(2)}) async-start(), calls=%async_computation.5 | async-start | bytes 2359296 | tf_op jit(solution)/shard_map/all_gather | solution.py:136
  56.4 3.4 copy-start
  246.9 5.4 %copy-start.9 = (f32[4096]{0:T(1024)S(1)}, f32[4096]{0:T(1024)}, u32[]{:S(2)}) copy-start(f32[4096]{0:T(1024)} %param.22) | copy-start | bytes 49156
  246.9 5.5 %copy-start.10 = (f32[4096]{0:T(1024)S(1)}, f32[4096]{0:T(1024)}, u32[]{:S(2)}) copy-start(f32[4096]{0:T(1024)} %param.21) | copy-start | bytes 49156
  246.9 5.5 %copy-start.13 = (f32[1024]{0:T(1024)S(1)}, f32[1024]{0:T(1024)}, u32[]{:S(2)}) copy-start(f32[1024]{0:T(1024)} %param.28) | copy-start | bytes 12292
  246.9 105.4 %all-to-all-start = ((bf16[9,2,16,16,256]{4,2,1,0,3:T(8,128)(2,1)}), bf16[9,2,16,16,256]{4,2,1,0,3:T(8,128)(2,1)S(1)}, u32[]{:S(2)}, u32[]{:S(2)}) async-start(bf16[9,2,16,16,256]{4,2,1,0,3:T(8,128)(2,1)} %bitcast.50), calls=%async_computation | async-start | bytes 4718592 | tf_op jit(solution)/shard_map/all_to_all | solution.py:73
  252.1 78.4 %copy-start.11 = (f32[4096]{0:T(1024)S(1)}, f32[4096]{0:T(1024)}, u32[]{:S(2)}) copy-start(f32[4096]{0:T(1024)} %param.20) | copy-start | bytes 49156
  252.1 78.4 %copy-start.12 = (f32[4096]{0:T(1024)S(1)}, f32[4096]{0:T(1024)}, u32[]{:S(2)}) copy-start(f32[4096]{0:T(1024)} %param.19) | copy-start | bytes 49156
  252.1 78.4 %copy-start.14 = (f32[768]{0:T(1024)S(1)}, f32[768]{0:T(1024)}, u32[]{:S(2)}) copy-start(f32[768]{0:T(1024)} %param.24) | copy-start | bytes 9220
  252.2 204.3 %reduce-scatter.2.cloned.1.call-start = ((), (), s32[]{:S(2)}) async-start(), calls=%async_computation.6 | async-start | bytes 4456448 | tf_op jit(solution)/shard_map/reduce_scatter | solution.py:144
  357.5 2.4 copy-start.1
  357.8 2.1 copy-start.2
  359.9 9.9 %copy-start.3 = (bf16[2048,2,128]{0,2,1:T(8,128)(2,1)S(1)}, bf16[2048,2,128]{0,2,1:T(8,128)(2,1)}, u32[]{:S(2)}) copy-start(bf16[2048,2,128]{0,2,1:T(8,128)(2,1)} %copy.46) | copy-start | bytes 3145732
  391.1 65.4 %copy-start.6 = (f32[256]{0:T(256)S(1)}, f32[256]{0:T(256)}, u32[]{:S(2)}) copy-start(f32[256]{0:T(256)} %param.30) | copy-start | bytes 3076
  391.1 65.4 %copy-start.7 = (f32[256]{0:T(256)S(1)}, f32[256]{0:T(256)}, u32[]{:S(2)}) copy-start(f32[256]{0:T(256)} %param.26) | copy-start | bytes 3076
Sparse Core Ops, SparseCore 0:
  9.0 47.3 all-gather.6
  58.1 170.7 all-gather.4
  231.2 99.2 all-gather.8
  332.6 51.2 all-gather.10
  391.3 65.1 reduce-scatter.1
